TPU v7x, 32 devices: a whole 2x2x4 slice. The times are simulated.
32 devices in a mesh: seq: 4 (over z), ch: 8 (over y, x, core).
Axes of the slice: x: 2, y: 2, z: 4, core: 2. Of those that a mesh axis runs over, the one named last changes fastest.
Arguments:
- inputs: bfloat16 [1024, 8192], P('seq', 'ch'), may hold values from -6 to 6
- w_in: bfloat16 [3, 8192, 8192], P(None, 'seq', 'ch'), may hold values from -0.0625 to 0.0625
- short_filter: float32 [3, 3, 8192], P(None, None, 'ch'), may hold values from -3 to 3
- rates: float32 [16, 8192], P(None, 'ch'), may hold values from 9.765625e-05 to 0.05
- residues: float32 [16, 8192], P(None, 'ch'), may hold values from -3 to 3
- skip: float32 [8192], P('ch'), may hold values from -3 to 3
Outputs:
- gated: bfloat16 [1024, 8192], P('seq', 'ch')
All inputs are finite; a program needn't handle non-finite values.
Results may differ from a plain program's by a relative error of at most 0.0065.
Values may be sent and summed in bfloat16 or wider, within the bound.
No kernel may reach another device: no remote copies, remote signals or barrier semaphores. Data moves between devices by JAX's collectives and lax.ppermute only.
A program may use at most 128 MiB of HBM per device.

v0:
```python
import jax
import jax.numpy as jnp
from jax import lax
from jax.sharding import PartitionSpec as P

TAPS = 3


def passed_along(block, axis, distance):
    devices = range(lax.axis_size(axis))
    route = [(i - distance, i) for i in devices if i - distance in devices]
    return lax.ppermute(block, axis, route)


def carried_in(end_state, decay, axis):
    total = lax.axis_size(axis)
    state = jnp.zeros_like(end_state)
    for distance in range(total - 1, 0, -1):
        state = state * decay + passed_along(end_state, axis, distance)
    return state


def project(inputs, w_in):
    tok_rows, local = inputs.shape
    n_seq = lax.axis_size("seq")
    n_ch = lax.axis_size("ch")
    share = tok_rows // n_ch
    pieces = lax.all_to_all(inputs.reshape(n_ch, share, local), "ch", 0, 0, tiled=True)
    pieces = pieces.transpose(1, 0, 2).reshape(share, n_seq, n_ch * local // n_seq)
    rows = lax.all_to_all(pieces, "seq", 1, 0, tiled=True)
    rows = rows.reshape(n_seq, share, rows.shape[-1])
    block = lax.all_gather(rows, "ch", axis=1, tiled=True)
    block = block.reshape(n_seq * tok_rows, block.shape[-1])
    partial = jnp.einsum("td,kdc->ktc", block, w_in, preferred_element_type=jnp.float32)
    return lax.psum_scatter(partial, "seq", scatter_dimension=1, tiled=True)


def per_device(inputs, w_in, short_filter, rates, residues, skip):
    tok_rows = inputs.shape[0]
    width = w_in.shape[2]
    modes = rates.shape[0]
    proj = project(inputs, w_in).astype(jnp.bfloat16)
    prior = passed_along(proj[:, tok_rows - (TAPS - 1) :, :], "seq", 1)
    padded = jnp.concatenate([prior, proj], axis=1).astype(jnp.float32)
    mixed = jnp.zeros((3, tok_rows, width), jnp.float32)
    for j in range(TAPS):
        mixed = (
            mixed
            + short_filter[:, j, None, :] * padded[:, TAPS - 1 - j : TAPS - 1 - j + tok_rows, :]
        )
    query, key, value = (mixed[0], mixed[1], mixed[2])
    drive = key * value
    position = jnp.arange(tok_rows, dtype=jnp.float32)
    scaled = residues * jnp.sqrt(1.0 - jnp.exp(-2.0 * rates))
    end_powers = jnp.exp(-rates[None, :, :] * (tok_rows - 1.0 - position)[:, None, None])
    end_state = jnp.sum(end_powers * drive[:, None, :], axis=0)
    block_decay = jnp.exp(-rates * tok_rows)
    entering = carried_in(end_state, block_decay, "seq")
    start_powers = jnp.exp(-rates[None, :, :] * (position + 1.0)[:, None, None])
    cross = jnp.sum(start_powers * (scaled * entering)[None, :, :], axis=1)
    center = (tok_rows - 1.0) / 2.0
    offset = (position - center)[:, None, None]
    rising = jnp.exp(rates[None, :, :] * offset) * drive[:, None, :]
    offsets = jnp.arange(tok_rows, dtype=jnp.int32)
    lower = (offsets[:, None] >= offsets[None, :]).astype(jnp.float32)
    prefix = jnp.dot(
        lower, rising.reshape(tok_rows, modes * width), precision=lax.Precision.HIGHEST
    )
    prefix = prefix.reshape(tok_rows, modes, width)
    falling = jnp.exp(-rates[None, :, :] * offset) * scaled[None, :, :]
    local = jnp.sum(falling * prefix, axis=1)
    return (query * (local + cross + skip[None, :] * drive)).astype(jnp.bfloat16)


def solution(mesh):
    in_specs = (
        P("seq", "ch"),
        P(None, "seq", "ch"),
        P(None, None, "ch"),
        P(None, "ch"),
        P(None, "ch"),
        P("ch"),
    )
    out_specs = P("seq", "ch")
    return jax.shard_map(
        per_device, mesh=mesh, in_specs=in_specs, out_specs=out_specs, check_vma=False
    )
```

profile of v0, /device:TPU:0, one launch (start us, length us, event | category | flops | bytes accessed | tf_op | source)
XLA Modules:
  0.0 379.0 jit_solution(15950338442145141932)
XLA Ops:
  6.5 0.0 all-gather.3.cloned.1.call-start
  6.5 14.9 %all_to_all.20 = bf16[8,32,1024]{2,1,0:T(8,128)(2,1)S(1)} all-to-all(bf16[8,32,1024]{2,1,0:T(8,128)(2,1)} %bitcast.45), channel_id=1, replica_groups=mesh['seq'=4,'ch'=8] {'ch'}, dimensions={0} | all-to-all | bytes 1048576 | tf_op jit(solution)/shard_map/all_to_all | solution.py:28
  21.4 0.3 copy.16
  21.7 0.4 reshape.48
  22.1 0.3 copy.17
  22.4 18.6 %all_to_all.21 = bf16[32,4,2048]{2,0,1:T(8,128)(2,1)S(1)} all-to-all(bf16[32,4,2048]{2,0,1:T(8,128)(2,1)S(1)} %copy.17), channel_id=1, replica_groups=mesh['seq'=4,'ch'=8] {'seq'}, dimensions={1} | all-to-all | bytes 1048576 | tf_op jit(solution)/shard_map/all_to_all | solution.py:30
  41.0 1.2 copy.18
  42.2 0.0 all-gather.3.cloned.1.call-update
  42.3 0.0 reduce-scatter.2.cloned.1.call-start
  42.3 34.5 %all-gather.3.cloned.1.call-done = bf16[4,256,1,2048]{3,0,2,1:T(4,128)(2,1)} async-done(((bf16[4,32,1,2048]{3,0,2,1:T(4,128)(2,1)}), bf16[4,256,1,2048]{3,0,2,1:T(4,128)(2,1)}) %all-gather.3.cloned.1.call-update) | async-done | bytes 4194320 | tf_op jit(solution)/shard_map/all_gather | solution.py:32
  76.8 4.5 %copy.19 = bf16[4,256,1,2048]{3,1,0,2:T(8,128)(2,1)S(1)} copy(bf16[4,256,1,2048]{3,0,2,1:T(4,128)(2,1)} %all-gather.3.cloned.1.call-done) | data formatting | bytes 8388608 | tf_op jit(solution)/shard_map/all_gather | solution.py:32
  81.3 17.8 %convolution_bitcast_fusion = f32[3,1024,1024]{1,2,0:T(8,128)} fusion(bf16[3,2048,1024]{2,1,0:T(8,128)(2,1)} %param.7, bf16[1024,2048,1]{1,0,2:T(8,128)(2,1)S(1)} %bitcast.41), kind=kOutput, calls=%fused_computation.4 | convolution fusion | flops 12884901888 | bytes 29360128 | tf_op jit(solution)/shard_map/td,kdc->ktc/dot_general | solution.py:34
  99.1 0.0 copy-start.2
  99.1 0.0 copy-start
  99.1 0.0 reduce-scatter.2.cloned.1.call-update
  99.2 0.8 copy-done.2
  100.0 211.2 %reduce-scatter.2.cloned.1.call-done = f32[3,256,1024]{1,2,0:T(8,128)} async-done(((f32[3,1024,1024]{1,2,0:T(8,128)}), f32[3,256,1024]{1,2,0:T(8,128)}) %reduce-scatter.2.cloned.1.call-update) | async-done | bytes 3145744 | tf_op jit(solution)/shard_map/reduce_scatter | solution.py:35
  311.2 2.0 convert_element_type.10
  313.2 0.3 slice.40
  313.5 0.3 copy.21
  313.8 3.6 collective-permute-start
  317.4 0.0 copy-done
  317.5 1.1 collective-permute-done
  318.6 0.4 copy.22
  319.0 1.0 maximum_convert_fusion
  320.0 3.2 fusion
  323.2 1.1 fusion.2
  324.3 2.6 copy.23
  326.9 0.0 copy-start.1
  326.9 4.2 %multiply_reduce_fusion.1 = f32[16,1024]{1,0:T(8,128)S(1)} fusion(f32[256]{0:T(256)S(1)} %iota_subtract_fusion, f32[256,1024]{1,0:T(8,128)} %copy.23, f32[16,1024]{1,0:T(8,128)S(1)} %neg.3), kind=kLoop, calls=%fused_computation.2 | loop fusion | flops 12566528 | bytes 1180672 | tf_op jit(solution)/shard_map/reduce_sum | solution.py:56
  331.0 5.8 %collective-permute-start.1 = (f32[16,1024]{1,0:T(8,128)S(1)}, f32[16,1024]{1,0:T(8,128)S(1)}, u32[]{:S(2)}, u32[]{:S(2)}) collective-permute-start(f32[16,1024]{1,0:T(8,128)S(1)} %multiply_reduce_fusion.1), channel_id=1, source_target_pairs={{0,24},{1,25},{2,26},{3,27},{4,28},{5,29},{6,30},{7,31}} | collective-permute-start | bytes 196616 | tf_op jit(solution)/shard_map/ppermute | solution.py:12
  336.9 1.3 collective-permute-start.2
  338.2 2.5 collective-permute-start.3
  340.7 3.8 bitcast_multiply_fusion
  344.5 0.0 collective-permute-done.1
  344.5 0.0 collective-permute-done.2
  344.5 0.0 collective-permute-done.3
  344.5 0.0 copy-done.1
  344.5 0.1 add_multiply_fusion
  344.6 0.0 copy-start.3
  344.6 14.1 %multiply_reduce_fusion.2 = f32[256,1024]{1,0:T(8,128)} fusion(f32[16,1024,256]{2,1,0:T(8,128)S(1)} %bitcast.40, f32[16,1024]{1,0:T(8,128)S(1)} %get-tuple-element.6, f32[256]{0:T(256)S(1)} %iota_add_fusion.1, f32[16,1024]{1,0:T(8,128)S(1)} %neg.3), kind=kOutput, calls=%fused_computation.3 | convolution fusion | flops 12901482496 | bytes 17957888 | tf_op jit(solution)/shard_map/dot_general | solution.py:66
  358.6 2.5 copy.25
  361.2 3.8 multiply_reduce_fusion
  364.9 2.6 copy.26
  367.5 0.0 copy-done.3
  367.5 2.6 fusion.4
  370.1 2.0 copy.27
  (8 shorter events, 0.1 us)
Async XLA Ops:
  6.5 70.3 %all-gather.3.cloned.1.call-start = ((), (), s32[]{:S(2)}) async-start(), calls=%async_computation.4 | async-start | bytes 4718592 | tf_op jit(solution)/shard_map/all_gather | solution.py:32
  42.3 268.9 %reduce-scatter.2.cloned.1.call-start = ((), (), s32[]{:S(2)}) async-start(), calls=%async_computation.3 | async-start | bytes 15728640 | tf_op jit(solution)/shard_map/reduce_scatter | solution.py:35
  99.1 0.8 copy-start.2
  99.1 218.3 %copy-start = (f32[16,1024]{1,0:T(8,128)S(1)}, f32[16,1024]{1,0:T(8,128)}, u32[]{:S(2)}) copy-start(f32[16,1024]{1,0:T(8,128)} %param.9) | copy-start | bytes 196612
  313.8 4.8 %collective-permute-start = (bf16[3,2,1024]{2,1,0:T(2,128)(2,1)S(1)}, bf16[3,2,1024]{2,1,0:T(2,128)(2,1)S(1)}, u32[]{:S(2)}, u32[]{:S(2)}) collective-permute-start(bf16[3,2,1024]{2,1,0:T(2,128)(2,1)S(1)} %copy.21), channel_id=1, source_target_pairs={{0,8},{8,16},{16,24},{1,9},{9,17},{17,25},{2,10},{10,18},{18,26},{... | collective-permute-start | bytes 36872 | tf_op jit(solution)/shard_map/ppermute | solution.py:12
  326.9 17.6 %copy-start.1 = (f32[16,1024]{1,0:T(8,128)S(1)}, f32[16,1024]{1,0:T(8,128)}, u32[]{:S(2)}) copy-start(f32[16,1024]{1,0:T(8,128)} %param.10) | copy-start | bytes 196612
  331.0 13.4 %collective-permute-start.1 = (f32[16,1024]{1,0:T(8,128)S(1)}, f32[16,1024]{1,0:T(8,128)S(1)}, u32[]{:S(2)}, u32[]{:S(2)}) collective-permute-start(f32[16,1024]{1,0:T(8,128)S(1)} %multiply_reduce_fusion.1), channel_id=1, source_target_pairs={{0,24},{1,25},{2,26},{3,27},{4,28},{5,29},{6,30},{7,31}} | collective-permute-start | bytes 196616 | tf_op jit(solution)/shard_map/ppermute | solution.py:12
  336.9 7.6 %collective-permute-start.2 = (f32[16,1024]{1,0:T(8,128)S(1)}, f32[16,1024]{1,0:T(8,128)S(1)}, u32[]{:S(2)}, u32[]{:S(2)}) collective-permute-start(f32[16,1024]{1,0:T(8,128)S(1)} %multiply_reduce_fusion.1), channel_id=1, source_target_pairs={{0,16},{8,24},{1,17},{9,25},{2,18},{10,26},{3,19},{11,27},{4,20},{... | collective-permute-start | bytes 196616 | tf_op jit(solution)/shard_map/ppermute | solution.py:12
  338.2 6.3 %collective-permute-start.3 = (f32[16,1024]{1,0:T(8,128)S(1)}, f32[16,1024]{1,0:T(8,128)S(1)}, u32[]{:S(2)}, u32[]{:S(2)}) collective-permute-start(f32[16,1024]{1,0:T(8,128)S(1)} %multiply_reduce_fusion.1), channel_id=1, source_target_pairs={{0,8},{8,16},{16,24},{1,9},{9,17},{17,25},{2,10},{10,18},{18,26},{... | collective-permute-start | bytes 196616 | tf_op jit(solution)/shard_map/ppermute | solution.py:12
  344.6 23.0 %copy-start.3 = (f32[1024]{0:T(1024)S(1)}, f32[1024]{0:T(1024)}, u32[]{:S(2)}) copy-start(f32[1024]{0:T(1024)} %param.11) | copy-start | bytes 12292
Sparse Core Ops, SparseCore 0:
  42.4 34.4 all-gather.2
  99.3 211.8 reduce-scatter.1
where the time goes:
time: 380 us; the launch traced here: 379 us
  waiting for transfers between devices  247 us (65%)
  blocking collectives  33.5 us (9%)
  matrix products  31.9 us (8%)
  other arithmetic  21.7 us (6%)
  local copies, waits for them, and re-layouts  18.2 us (5%)
  between operations  13.6 us (4%)
  starting transfers between devices  13.2 us (3%)
    reduce_scatter x1, waiting for transfers between devices, project(): return lax.psum_scatter(partial, 'seq', scatter_dimension=1, tiled=True)  211 us
    all_gather x1, waiting for transfers between devices, project(): block = lax.all_gather(rows, 'ch', axis=1, tiled=True)  34.5 us
    all_to_all x1, blocking collectives, project(): rows = lax.all_to_all(pieces, 'seq', 1, 0, tiled=True)  18.6 us
    dot_general x1, matrix products, project(): jnp.einsum('td,kdc->ktc', block, w_in, preferred_element_type=jnp.float32)  17.8 us
    all_to_all x1, blocking collectives, project(): lax.all_to_all(inputs.reshape(n_ch, share, local), 'ch', 0, 0, tiled=True)  14.9 us
    dot_general x1, matrix products, per_device(): jnp.dot(lower, rising.reshape(tok_rows, modes * width), precision=lax.Pre...  14.1 us
    ppermute x4, starting transfers between devices, passed_along(): return lax.ppermute(block, axis, route)  13.2 us
  transfers between devices with their start and end apart: 6, of which 3 were waited for; matrix products, arithmetic and copies ran while one was open for 1% of the time, Pallas kernels for 0%

commit v1 on v0

--- a/solution.py
+++ b/solution.py
@@ -1,9 +1,21 @@
+import functools
 import jax
 import jax.numpy as jnp
 from jax import lax
 from jax.sharding import PartitionSpec as P
 
 TAPS = 3
+
+
+def obtain_vector(patch, a_name, dim_i, on_dim):
+    r2 = lax.axis_size(a_name)
+    near = jnp.stack(jnp.split(patch, r2, axis=dim_i))
+    next_value = lax.all_to_all(near, a_name, 0, 0)
+    x_new = jnp.concatenate(next_value, axis=on_dim)
+    return x_new
+
+
+report_outputs_on = functools.partial(obtain_vector, a_name="seq", dim_i=1, on_dim=0)
 
 
 def passed_along(block, axis, distance):
@@ -27,7 +39,7 @@
     share = tok_rows // n_ch
     pieces = lax.all_to_all(inputs.reshape(n_ch, share, local), "ch", 0, 0, tiled=True)
     pieces = pieces.transpose(1, 0, 2).reshape(share, n_seq, n_ch * local // n_seq)
-    rows = lax.all_to_all(pieces, "seq", 1, 0, tiled=True)
+    rows = report_outputs_on(pieces)
     rows = rows.reshape(n_seq, share, rows.shape[-1])
     block = lax.all_gather(rows, "ch", axis=1, tiled=True)
     block = block.reshape(n_seq * tok_rows, block.shape[-1])

time: 380 us -> 364 us (0.958)
  local copies, waits for them, and re-layouts: 18.2 us -> 6.13 us
  other arithmetic: 21.7 us -> 16.5 us
    reduce_sum x2 -> x0, local copies, waits for them, and re-layouts: 5.12 us -> none  [the longest x1 2.58 us: per_device(): cross = jnp.sum(start_powers * (scaled * entering)[None, :, :], axis=1)]
    all_gather x1 -> x0, local copies, waits for them, and re-layouts: 4.48 us -> none  [project(): block = lax.all_gather(rows, 'ch', axis=1, tiled=True)]
    unnamed x11 -> x20, local copies, waits for them, and re-layouts: 0.8 us -> 4.64 us
  transfers between devices with their start and end apart: 6 -> 6, of which waited for: 3 -> 3; matrix products, arithmetic and copies ran while one was open for 1% -> 2% of each run, Pallas kernels for 0% -> 0%
where the time goes in v1:
time: 364 us; the launch traced here: 363 us
  waiting for transfers between devices  247 us (68%)
  blocking collectives  33.6 us (9%)
  matrix products  33 us (9%)
  other arithmetic  16.5 us (5%)
  between operations  13.7 us (4%)
  starting transfers between devices  13.2 us (4%)
  local copies, waits for them, and re-layouts  6.13 us (2%)
    reduce_scatter x1, waiting for transfers between devices, project(): return lax.psum_scatter(partial, 'seq', scatter_dimension=1, tiled=True)  211 us
    all_gather x1, waiting for transfers between devices, project(): block = lax.all_gather(rows, 'ch', axis=1, tiled=True)  34.5 us
    dot_general x1, matrix products, project(): jnp.einsum('td,kdc->ktc', block, w_in, preferred_element_type=jnp.float32)  18.9 us
    all_to_all x1, blocking collectives, obtain_vector(): next_value = lax.all_to_all(near, a_name, 0, 0)  18.7 us
    all_to_all x1, blocking collectives, project(): lax.all_to_all(inputs.reshape(n_ch, share, local), 'ch', 0, 0, tiled=True)  14.9 us
    dot_general x1, matrix products, per_device(): jnp.dot(lower, rising.reshape(tok_rows, modes * width), precision=lax.Pre...  14 us
    ppermute x4, starting transfers between devices, passed_along(): return lax.ppermute(block, axis, route)  13.2 us
  transfers between devices with their start and end apart: 6, of which 3 were waited for; matrix products, arithmetic and copies ran while one was open for 2% of the time, Pallas kernels for 0%

profile of v1, /device:TPU:0, one launch (start us, length us, event | category | flops | bytes accessed | tf_op | source)
XLA Modules:
  0.0 363.2 jit_solution(11586986080674037661)
XLA Ops:
  6.5 0.0 all-gather.3.cloned.1.call-start
  6.5 14.9 %all_to_all.10 = bf16[8,32,1024]{2,1,0:T(8,128)(2,1)S(1)} all-to-all(bf16[8,32,1024]{2,1,0:T(8,128)(2,1)} %bitcast.48), channel_id=1, replica_groups=mesh['seq'=4,'ch'=8] {'ch'}, dimensions={0} | all-to-all | bytes 1048576 | tf_op jit(solution)/shard_map/all_to_all | solution.py:40
  21.4 0.3 copy.26
  21.7 0.4 reshape.44
  22.1 0.8 fusion.7
  22.9 0.2 copy_bitcast_fusion
  23.1 0.2 copy_bitcast_fusion.2
  23.2 0.1 pad_maximum_fusion
  23.3 18.7 %all_to_all.11 = bf16[4,32,1,2048]{3,1,2,0:T(8,128)(2,1)} all-to-all(bf16[4,32,1,2048]{3,1,2,0:T(8,128)(2,1)S(1)} %pad_maximum_fusion), channel_id=1, replica_groups=mesh['seq'=4,'ch'=8] {'seq'}, dimensions={0} | all-to-all | bytes 1048576 | tf_op jit(solution)/shard_map/all_to_all | solution.py:13
  42.0 0.0 all-gather.3.cloned.1.call-update
  42.0 0.0 reduce-scatter.2.cloned.1.call-start
  42.1 34.5 %all-gather.3.cloned.1.call-done = bf16[4,256,1,2048]{3,1,2,0:T(8,128)(2,1)} async-done(((bf16[4,32,1,2048]{3,1,2,0:T(8,128)(2,1)}), bf16[4,256,1,2048]{3,1,2,0:T(8,128)(2,1)}) %all-gather.3.cloned.1.call-update) | async-done | bytes 4194320 | tf_op jit(solution)/shard_map/all_gather | solution.py:44
  76.6 18.9 %convolution_bitcast_fusion = f32[3,1024,1024]{2,1,0:T(8,128)} fusion(bf16[1024,2048,1]{1,0,2:T(8,128)(2,1)} %bitcast.51, bf16[3,2048,1024]{2,1,0:T(8,128)(2,1)} %param.7), kind=kOutput, calls=%fused_computation.4 | convolution fusion | flops 12884901888 | bytes 29360128 | tf_op jit(solution)/shard_map/td,kdc->ktc/dot_general | solution.py:46
  95.5 0.0 copy-start.5
  95.5 0.0 copy-start.1
  95.5 0.0 reduce-scatter.2.cloned.1.call-update
  95.6 0.8 copy-done.5
  96.4 211.2 %reduce-scatter.2.cloned.1.call-done = f32[3,256,1024]{2,1,0:T(8,128)} async-done(((f32[3,1024,1024]{2,1,0:T(8,128)}), f32[3,256,1024]{2,1,0:T(8,128)}) %reduce-scatter.2.cloned.1.call-update) | async-done | bytes 3145744 | tf_op jit(solution)/shard_map/reduce_scatter | solution.py:47
  307.6 2.1 convert_element_type.10
  309.7 3.4 collective-permute-start
  313.2 0.0 copy-done.1
  313.2 0.0 copy-start.3
  313.2 1.3 collective-permute-done
  314.5 0.5 maximum_convert_fusion
  315.0 0.9 fusion
  315.9 0.1 fusion.2
  316.1 0.0 copy-start
  316.1 1.0 copy-done
  317.1 0.0 copy-start.2
  317.1 3.5 multiply_reduce_fusion.1
  320.6 0.0 copy-done.3
  320.6 4.4 %collective-permute-start.3 = (f32[16,1024]{1,0:T(8,128)}, f32[16,1024]{1,0:T(8,128)S(1)}, u32[]{:S(2)}, u32[]{:S(2)}) collective-permute-start(f32[16,1024]{1,0:T(8,128)} %multiply_reduce_fusion.1), channel_id=1, source_target_pairs={{0,8},{8,16},{16,24},{1,9},{9,17},{17,25},{2,10},{10,18},{18,26},{... | collective-permute-start | bytes 196616 | tf_op jit(solution)/shard_map/ppermute | solution.py:24
  325.0 3.9 %collective-permute-start.2 = (f32[16,1024]{1,0:T(8,128)}, f32[16,1024]{1,0:T(8,128)S(1)}, u32[]{:S(2)}, u32[]{:S(2)}) collective-permute-start(f32[16,1024]{1,0:T(8,128)} %multiply_reduce_fusion.1), channel_id=1, source_target_pairs={{0,16},{8,24},{1,17},{9,25},{2,18},{10,26},{3,19},{11,27},{4,20},{... | collective-permute-start | bytes 196616 | tf_op jit(solution)/shard_map/ppermute | solution.py:24
  328.9 1.5 collective-permute-start.1
  330.4 2.6 copy.36
  333.0 0.0 copy-start.4
  333.0 3.8 %bitcast_multiply_fusion = f32[256,16384]{0,1:T(8,128)S(1)} fusion(f32[256,1024]{0,1:T(8,128)} %copy.36, f32[256]{0:T(256)S(1)} %iota_add_fusion.1, f32[16384]{0:T(1024)S(1)} %bitcast.49), kind=kLoop, calls=%fused_computation | loop fusion | flops 8388608 | bytes 17892352 | tf_op jit(solution)/shard_map/mul | solution.py:75
  336.8 0.0 collective-permute-done.3
  336.8 0.0 collective-permute-done.2
  336.8 0.0 collective-permute-done.1
  336.8 0.0 copy-done.2
  336.8 0.1 add_multiply_fusion
  336.9 0.0 copy-done.4
  336.9 0.0 copy-start.6
  336.9 14.0 %multiply_reduce_fusion.2 = f32[256,1024]{1,0:T(8,128)} fusion(f32[16,1024,256]{2,1,0:T(8,128)S(1)} %bitcast.45, f32[16,1024]{1,0:T(8,128)S(1)} %get-tuple-element.6, f32[256]{0:T(256)S(1)} %iota_add_fusion.1, f32[16,1024]{1,0:T(8,128)S(1)} %copy-done.4), kind=kOutput, calls=%fused_computation.3 | convolution fusion | flops 12901482496 | bytes 17957888 | tf_op jit(solution)/shard_map/dot_general | solution.py:78
  350.9 2.8 multiply_reduce_fusion
  353.7 0.0 copy-done.6
  353.7 2.6 fusion.4
  (9 shorter events, 0.1 us)
Async XLA Ops:
  6.5 70.1 %all-gather.3.cloned.1.call-start = ((), (), s32[]{:S(2)}) async-start(), calls=%async_computation.4 | async-start | bytes 4718592 | tf_op jit(solution)/shard_map/all_gather | solution.py:44
  42.0 265.5 %reduce-scatter.2.cloned.1.call-start = ((), (), s32[]{:S(2)}) async-start(), calls=%async_computation.3 | async-start | bytes 15728640 | tf_op jit(solution)/shard_map/reduce_scatter | solution.py:47
  95.5 0.8 copy-start.5
  95.5 217.6 %copy-start.1 = (f32[16,1024]{1,0:T(8,128)S(1)}, f32[16,1024]{1,0:T(8,128)}, u32[]{:S(2)}) copy-start(f32[16,1024]{1,0:T(8,128)} %param.9) | copy-start | bytes 196612
  309.7 4.8 %collective-permute-start = (bf16[3,2,1024]{2,1,0:T(2,128)(2,1)S(1)}, bf16[3,2,1024]{2,1,0:T(2,128)(2,1)S(1)}, u32[]{:S(2)}, u32[]{:S(2)}) collective-permute-start(bf16[3,2,1024]{2,1,0:T(2,128)(2,1)S(1)} %slice.40), channel_id=1, source_target_pairs={{0,8},{8,16},{16,24},{1,9},{9,17},{17,25},{2,10},{10,18},{18,26},{... | collective-permute-start | bytes 36872 | tf_op jit(solution)/shard_map/ppermute | solution.py:24
  313.2 7.4 %copy-start.3 = (f32[16,1024]{1,0:T(8,128)}, f32[16,1024]{1,0:T(8,128)S(1)}, u32[]{:S(2)}) copy-start(f32[16,1024]{1,0:T(8,128)S(1)} %neg.3) | copy-start | bytes 196612
  316.1 1.0 copy-start
  317.1 19.7 %copy-start.2 = (f32[16,1024]{1,0:T(8,128)S(1)}, f32[16,1024]{1,0:T(8,128)}, u32[]{:S(2)}) copy-start(f32[16,1024]{1,0:T(8,128)} %param.10) | copy-start | bytes 196612
  320.6 16.2 %collective-permute-start.3 = (f32[16,1024]{1,0:T(8,128)}, f32[16,1024]{1,0:T(8,128)S(1)}, u32[]{:S(2)}, u32[]{:S(2)}) collective-permute-start(f32[16,1024]{1,0:T(8,128)} %multiply_reduce_fusion.1), channel_id=1, source_target_pairs={{0,8},{8,16},{16,24},{1,9},{9,17},{17,25},{2,10},{10,18},{18,26},{... | collective-permute-start | bytes 196616 | tf_op jit(solution)/shard_map/ppermute | solution.py:24
  325.0 11.7 %collective-permute-start.2 = (f32[16,1024]{1,0:T(8,128)}, f32[16,1024]{1,0:T(8,128)S(1)}, u32[]{:S(2)}, u32[]{:S(2)}) collective-permute-start(f32[16,1024]{1,0:T(8,128)} %multiply_reduce_fusion.1), channel_id=1, source_target_pairs={{0,16},{8,24},{1,17},{9,25},{2,18},{10,26},{3,19},{11,27},{4,20},{... | collective-permute-start | bytes 196616 | tf_op jit(solution)/shard_map/ppermute | solution.py:24
  328.9 7.9 %collective-permute-start.1 = (f32[16,1024]{1,0:T(8,128)}, f32[16,1024]{1,0:T(8,128)S(1)}, u32[]{:S(2)}, u32[]{:S(2)}) collective-permute-start(f32[16,1024]{1,0:T(8,128)} %multiply_reduce_fusion.1), channel_id=1, source_target_pairs={{0,24},{1,25},{2,26},{3,27},{4,28},{5,29},{6,30},{7,31}} | collective-permute-start | bytes 196616 | tf_op jit(solution)/shard_map/ppermute | solution.py:24
  333.0 3.9 %copy-start.4 = (f32[16,1024]{1,0:T(8,128)S(1)}, f32[16,1024]{1,0:T(8,128)}, u32[]{:S(2)}) copy-start(f32[16,1024]{1,0:T(8,128)} %copy-done.3) | copy-start | bytes 196612
  336.9 16.8 %copy-start.6 = (f32[1024]{0:T(1024)S(1)}, f32[1024]{0:T(1024)}, u32[]{:S(2)}) copy-start(f32[1024]{0:T(1024)} %param.11) | copy-start | bytes 12292
Sparse Core Ops, SparseCore 0:
  42.2 34.4 all-gather.2
  95.7 211.8 reduce-scatter.1
